TPU v7x, 32 devices: a whole 2x2x4 slice. The times are simulated.
32 devices in a mesh: case: 2 (over y), tm: 4 (over z), bundle: 2 (over x), sub: 2 (over core).
Axes of the slice: x: 2, y: 2, z: 4, core: 2. Of those that a mesh axis runs over, the one named last changes fastest.
Arguments:
- cotangent: bfloat16 [16384, 512], P(('case', 'tm'), 'bundle'), parts along dimension 0, may hold values from -28 to 28
- inputs: bfloat16 [16384, 512], P(('case', 'tm'), 'bundle'), parts along dimension 0, may hold values from -6 to 6
- impulse: bfloat16 [8, 128, 4096], P('bundle', 'sub'), may hold values from -0.0625 to 0.0625
- terminal: int32 [8, 64], P('bundle'), may hold values from 0 to 63, each once within a row
- fault_step: int32 [2], P('case'), parts along dimension 0, may hold values from 0 to 4095
Outputs:
- voltage_grad: bfloat16 [16384, 512], P(('case', 'tm', 'sub'), 'bundle'), parts along dimension 0
- impulse_grad: float32 [16, 128, 4096], P(('case', 'bundle'), 'sub', 'tm'), parts along dimension 0
There are 2 independent parts, one for each index of `case`. A program takes and returns all parts, laid end to end along the dimension named above; an argument that names none is the same for every part. Nothing has to cross between parts.
Inputs may be any that keep to these rules, and one draw needn't show every extreme that they name: Each row of terminal orders the 64 terminals of a bundle, each once.
All inputs are finite; a program needn't handle non-finite values.
Results may differ from a plain program's by a relative error of at most 0.001.
Values may be sent and summed in bfloat16 or wider, within the bound.
No kernel may reach another device: no remote copies, remote signals or barrier semaphores. Data moves between devices by JAX's collectives and lax.ppermute only.
A program may use at most 320 MiB of HBM per device.

v0:
```python
import math
import jax
import jax.numpy as jnp
from jax import lax
from jax.sharding import PartitionSpec as P

CB = 64
NB = 8
L = 128
norm_ratio = 0.5
tile_rows = 8


def passed_along(block, axis, distance):
    devices = range(lax.axis_size(axis))
    route = [(i - distance, i) for i in devices if i - distance in devices]
    return lax.ppermute(block, axis, route)


def tiles_of(source, start, block_rows, lag_count):
    bundles = source.shape[0]
    width = source.shape[2]
    window = lax.dynamic_slice_in_dim(source, start, block_rows + lag_count, 1)
    tiled = window.reshape(bundles, (block_rows + lag_count) // tile_rows, tile_rows, width)
    tile_count = block_rows // tile_rows
    spans = [tiled[:, first : first + tile_count] for first in range(lag_count // tile_rows + 1)]
    wide = jnp.concatenate(spans, axis=2)
    return wide.reshape(bundles, tile_count, (lag_count + tile_rows) * width)


def local(cotangent, inputs, impulse, terminal, fault_step):
    seg_rows = cotangent.shape[0]
    local_bundles = terminal.shape[0]
    bundle_width = terminal.shape[1]
    lag_count = impulse.shape[1]
    all_lags = lag_count * lax.axis_size("sub")
    lag_first = lax.axis_index("sub") * lag_count
    columns = jnp.arange(bundle_width, dtype=jnp.int32)
    onehot = (terminal[:, :, None] == columns[None, None, :]).astype(jnp.bfloat16)
    grad_in = cotangent.reshape(seg_rows, local_bundles, bundle_width)
    reordered = jnp.einsum(
        "tbi,bir->tbr", grad_in, onehot, preferred_element_type=jnp.float32
    ).astype(jnp.bfloat16)
    seg_start = lax.axis_index("tm") * seg_rows
    steps_here = seg_start + jnp.arange(seg_rows, dtype=jnp.int32)
    live_rows = steps_here >= fault_step[0]
    masked = jnp.where(
        live_rows[:, None, None],
        inputs.reshape(seg_rows, local_bundles, bundle_width),
        jnp.zeros((), jnp.bfloat16),
    )
    ahead_rows = passed_along(reordered[:all_lags], "tm", -1)
    extended = jnp.concatenate([reordered, ahead_rows], axis=0)
    ext_lanes = jnp.transpose(extended, (1, 0, 2))
    reord_lanes = jnp.transpose(reordered, (1, 0, 2))
    kernel = impulse.reshape(local_bundles, lag_count, bundle_width, bundle_width)
    zero_pad = jnp.zeros((local_bundles, tile_rows, bundle_width, bundle_width), jnp.bfloat16)
    kernel_pad = jnp.concatenate([zero_pad, kernel, zero_pad], axis=1)
    toeplitz = jnp.stack(
        [
            kernel_pad[:, tile_rows - shift_row : tile_rows - shift_row + lag_count + tile_rows]
            for shift_row in range(tile_rows)
        ],
        axis=3,
    )
    toeplitz = toeplitz.reshape(
        local_bundles, (lag_count + tile_rows) * bundle_width, tile_rows * bundle_width
    )
    block_rows = min(512, seg_rows)
    block_count = seg_rows // block_rows
    tile_count = block_rows // tile_rows
    behind = passed_along(masked[seg_rows - all_lags :], "tm", 1)
    history = jnp.concatenate([behind, masked], axis=0)
    hist_lanes = jnp.transpose(history, (1, 0, 2))

    def advance(grad_acc, block_index):
        row_start = block_index * block_rows
        wide = tiles_of(ext_lanes, row_start + lag_first, block_rows, lag_count)
        dx_block = jnp.einsum("bkx,bxy->bky", wide, toeplitz, preferred_element_type=jnp.float32)
        row_block = lax.dynamic_slice_in_dim(reord_lanes, row_start, block_rows, 1).reshape(
            local_bundles, tile_count, tile_rows * bundle_width
        )
        earlier = tiles_of(
            hist_lanes, row_start + all_lags - lag_first - lag_count, block_rows, lag_count
        )
        grad_acc = grad_acc + jnp.einsum(
            "bkx,bky->bxy", row_block, earlier, preferred_element_type=jnp.float32
        )
        return (grad_acc, dx_block.reshape(local_bundles, block_rows, bundle_width))

    acc_shape = (local_bundles, tile_rows * bundle_width, (lag_count + tile_rows) * bundle_width)
    grad_total, dx_blocks = lax.scan(
        advance, jnp.zeros(acc_shape, jnp.float32), jnp.arange(block_count, dtype=jnp.int32)
    )
    partial_dx = jnp.transpose(dx_blocks, (0, 2, 1, 3)).reshape(
        seg_rows, local_bundles * bundle_width
    )
    folded = grad_total.reshape(
        local_bundles, tile_rows, bundle_width, lag_count + tile_rows, bundle_width
    )
    lag_sum = folded[:, 0, :, 1 : lag_count + 1, :]
    for shift_row in range(1, tile_rows):
        lag_sum = lag_sum + folded[:, shift_row, :, shift_row + 1 : shift_row + lag_count + 1, :]
    grad_blocks = jnp.transpose(jnp.flip(lag_sum, axis=2), (0, 2, 1, 3))
    summed_dx = lax.psum_scatter(partial_dx, "sub", scatter_dimension=0, tiled=True)
    share_rows = summed_dx.shape[0]
    own_steps = (
        seg_start + lax.axis_index("sub") * share_rows + jnp.arange(share_rows, dtype=jnp.int32)
    )
    voltage_grad = jnp.where((own_steps >= fault_step[0])[:, None], summed_dx, 0.0).astype(
        jnp.bfloat16
    )
    grad_flat = grad_blocks.reshape(local_bundles, lag_count, bundle_width * bundle_width)
    grad_sum = lax.psum(grad_flat, "tm")
    share_cols = grad_flat.shape[2] // lax.axis_size("tm")
    own_grad = lax.dynamic_slice_in_dim(grad_sum, lax.axis_index("tm") * share_cols, share_cols, 2)
    own_squares = jnp.sum(own_grad * own_grad)
    total_squares = lax.psum(own_squares, ("tm", "bundle", "sub"))
    norm_limit = norm_ratio * math.sqrt(NB * L * CB * CB)
    factor = norm_limit / jnp.sqrt(total_squares + 1e-06)
    return (voltage_grad, own_grad * factor)


def solution(mesh):
    placed = (
        P(("case", "tm"), "bundle"),
        P(("case", "tm"), "bundle"),
        P("bundle", "sub", None),
        P("bundle", None),
        P("case"),
    )
    return jax.shard_map(
        local,
        mesh=mesh,
        in_specs=placed,
        out_specs=(P(("case", "tm", "sub"), "bundle"), P(("case", "bundle"), "sub", "tm")),
        check_vma=False,
    )
```

profile of v0, /device:TPU:0, one launch (start us, length us, event | category | flops | bytes accessed | tf_op | source)
XLA Modules:
  0.0 749.6 jit_solution(2607385197991196513)
XLA Ops:
  59.8 47.4 %copy.50 = bf16[4,72,64,8,64]{4,3,2,1,0:T(8,128)(2,1)} copy(bf16[4,72,64,8,64]{1,4,3,2,0:T(8,128)(2,1)} %fusion.1) | data formatting | bytes 37748736 | tf_op jit(solution)/shard_map/stack | solution.py:59
  107.2 49.1 %reshape.92 = bf16[4,4608,512]{2,1,0:T(8,128)(2,1)} reshape(bf16[4,72,64,8,64]{4,3,2,1,0:T(8,128)(2,1)} %copy.50) | data formatting | bytes 37748736 | tf_op jit(solution)/shard_map/reshape | solution.py:66
  159.7 269.9 %while.17 = (s32[]{:T(128)}, f32[4,512,4608]{2,1,0:T(8,128)}, f32[4,4,512,64]{3,2,1,0:T(8,128)}, s32[4]{0:T(128)S(1)}, bf16[4,2048,64]{1,2,0:T(8,128)(2,1)}, /*i...) while((s32[]{:T(128)}, f32[4,512,4608]{2,1,0:T(8,128)}, ...), condition=%wide.region_1.2_spmd.clone, body=%wide.region_0.1_spmd.clone.sunk | while | flops 2434793472 | bytes 131072384 | solution.py:92
  173.4 6.1 reshape.109
  179.5 8.1 %fusion.24 = f32[4,64,512]{2,1,0:T(8,128)S(1)} fusion(bf16[4,64,4608]{2,1,0:T(8,128)(2,1)S(1)} %reshape.109, bf16[4,4608,512]{2,1,0:T(8,128)(2,1)} %get-tuple-element.366), kind=kOutput, calls=%fused_computation.58.clone.1 | convolution fusion | flops 1207959552 | bytes 21757952 | tf_op jit(solution)/shard_map/while/body/eval_jaxpr/bkx,bxy->bky/dot_general | solution.py:79
  196.9 6.1 reshape.108
  203.1 14.0 %select_add_fusion.2 = f32[4,512,4608]{2,1,0:T(8,128)} fusion(f32[4,512,4608]{2,1,0:T(8,128)} %get-tuple-element.342, pred[]{:T(512)S(6)} %compare.4, bf16[4,64,512]{2,1,0:T(8,128)(2,1)S(1)} %copy-done.1, bf16[4,64,4608]{2,1,0:T(8,128)(2,1)S(1)} %reshape.108), kind=kOutput, calls=%fused_computation.clone.1 | convolution fusion | flops 1226833920 | bytes 78118912 | tf_op jit(solution)/shard_map/while/body/eval_jaxpr/bkx,bky->bxy/dot_general | solution.py:86
  230.8 6.1 reshape.109
  236.9 8.1 %fusion.24 = f32[4,64,512]{2,1,0:T(8,128)S(1)} fusion(bf16[4,64,4608]{2,1,0:T(8,128)(2,1)S(1)} %reshape.109, bf16[4,4608,512]{2,1,0:T(8,128)(2,1)} %get-tuple-element.366), kind=kOutput, calls=%fused_computation.58.clone.1 | convolution fusion | flops 1207959552 | bytes 21757952 | tf_op jit(solution)/shard_map/while/body/eval_jaxpr/bkx,bxy->bky/dot_general | solution.py:79
  254.4 6.1 reshape.108
  260.5 27.4 %select_add_fusion.2 = f32[4,512,4608]{2,1,0:T(8,128)} fusion(f32[4,512,4608]{2,1,0:T(8,128)} %get-tuple-element.342, pred[]{:T(512)S(6)} %compare.4, bf16[4,64,512]{2,1,0:T(8,128)(2,1)S(1)} %copy-done.1, bf16[4,64,4608]{2,1,0:T(8,128)(2,1)S(1)} %reshape.108), kind=kOutput, calls=%fused_computation.clone.1 | convolution fusion | flops 1226833920 | bytes 78118912 | tf_op jit(solution)/shard_map/while/body/eval_jaxpr/bkx,bky->bxy/dot_general | solution.py:86
  301.6 6.1 reshape.109
  307.8 8.1 %fusion.24 = f32[4,64,512]{2,1,0:T(8,128)S(1)} fusion(bf16[4,64,4608]{2,1,0:T(8,128)(2,1)S(1)} %reshape.109, bf16[4,4608,512]{2,1,0:T(8,128)(2,1)} %get-tuple-element.366), kind=kOutput, calls=%fused_computation.58.clone.1 | convolution fusion | flops 1207959552 | bytes 21757952 | tf_op jit(solution)/shard_map/while/body/eval_jaxpr/bkx,bxy->bky/dot_general | solution.py:79
  331.4 27.4 %select_add_fusion.2 = f32[4,512,4608]{2,1,0:T(8,128)} fusion(f32[4,512,4608]{2,1,0:T(8,128)} %get-tuple-element.342, pred[]{:T(512)S(6)} %compare.4, bf16[4,64,512]{2,1,0:T(8,128)(2,1)S(1)} %copy-done.1, bf16[4,64,4608]{2,1,0:T(8,128)(2,1)S(1)} %reshape.108), kind=kOutput, calls=%fused_computation.clone.1 | convolution fusion | flops 1226833920 | bytes 78118912 | tf_op jit(solution)/shard_map/while/body/eval_jaxpr/bkx,bky->bxy/dot_general | solution.py:86
  378.6 8.1 %fusion.24 = f32[4,64,512]{2,1,0:T(8,128)S(1)} fusion(bf16[4,64,4608]{2,1,0:T(8,128)(2,1)S(1)} %reshape.109, bf16[4,4608,512]{2,1,0:T(8,128)(2,1)} %get-tuple-element.366), kind=kOutput, calls=%fused_computation.58.clone.1 | convolution fusion | flops 1207959552 | bytes 21757952 | tf_op jit(solution)/shard_map/while/body/eval_jaxpr/bkx,bxy->bky/dot_general | solution.py:79
  396.0 6.1 reshape.108
  402.2 27.4 %select_add_fusion.2 = f32[4,512,4608]{2,1,0:T(8,128)} fusion(f32[4,512,4608]{2,1,0:T(8,128)} %get-tuple-element.342, pred[]{:T(512)S(6)} %compare.4, bf16[4,64,512]{2,1,0:T(8,128)(2,1)S(1)} %copy-done.1, bf16[4,64,4608]{2,1,0:T(8,128)(2,1)S(1)} %reshape.108), kind=kOutput, calls=%fused_computation.clone.1 | convolution fusion | flops 1226833920 | bytes 78118912 | tf_op jit(solution)/shard_map/while/body/eval_jaxpr/bkx,bky->bxy/dot_general | solution.py:86
  435.6 54.3 %reshape.94 = f32[4,8,64,72,64]{4,3,2,1,0:T(8,128)} reshape(f32[4,512,4608]{2,1,0:T(8,128)} %get-tuple-element.183) | data formatting | bytes 75497472 | tf_op jit(solution)/shard_map/reshape | solution.py:98
  489.9 27.4 %fusion = f32[4,64,64,64]{3,2,1,0:T(8,128)} fusion(f32[4,8,64,72,64]{4,3,2,1,0:T(8,128)} %reshape.94), kind=kLoop, calls=%fused_computation.24 | loop fusion | flops 7340032 | bytes 37748736 | tf_op jit(solution)/shard_map/add | solution.py:103
  517.3 11.9 %rev.4 = f32[4,64,64,64]{3,2,1,0:T(8,128)} reverse(f32[4,64,64,64]{3,2,1,0:T(8,128)} %fusion), dimensions={2} | reverse | bytes 8388608 | tf_op jit(solution)/shard_map/jit(_flip)/rev | solution.py:104
  529.1 11.5 %copy.55 = f32[4,64,64,64]{3,2,1,0:T(8,128)} copy(f32[4,64,64,64]{3,1,2,0:T(8,128)} %bitcast.113) | data formatting | bytes 8388608 | tf_op jit(solution)/shard_map/transpose | solution.py:104
  540.6 7.9 %reshape.95 = f32[4,64,4096]{2,1,0:T(8,128)} reshape(f32[4,64,64,64]{3,2,1,0:T(8,128)} %copy.55) | data formatting | bytes 8388608 | tf_op jit(solution)/shard_map/reshape | solution.py:113
  549.9 154.3 %all-reduce.3.cloned.1.call-done = f32[4,64,4096]{2,1,0:T(8,128)} async-done(((f32[4,64,4096]{2,1,0:T(8,128)}), f32[4,64,4096]{2,1,0:T(8,128)}) %all-reduce.3.cloned.1.call-update) | async-done | bytes 4194320 | tf_op jit(solution)/shard_map/psum | solution.py:114
  707.3 31.9 %psum.15 = f32[]{:T(128)} all-reduce(f32[]{:T(128)} %multiply_reduce_fusion), channel_id=1, replica_groups=mesh['case'=2,'tm'=4,'bundle'=2,'sub'=2] {'tm','bundle','sub'}, use_global_device_ids=true, to_apply=%region_5.6 | all-reduce | flops 1 | bytes 8 | tf_op jit(solution)/shard_map/psum | solution.py:118
  (161 shorter events, 168.4 us)
Async XLA Ops:
  8.0 6.5 copy-start.2
  8.0 540.5 %reduce-scatter.2.cloned.1.call-start = ((), (), s32[]{:S(2)}) async-start(), calls=%async_computation.1 | async-start | bytes 3145728 | tf_op jit(solution)/shard_map/reduce_scatter | solution.py:105
  12.5 143.7 %collective-permute-start.1 = (bf16[128,4,64]{0,2,1:T(8,128)(2,1)S(1)}, bf16[128,4,64]{0,2,1:T(8,128)(2,1)S(1)}, u32[]{:S(2)}, u32[]{:S(2)}) collective-permute-start(bf16[128,4,64]{0,2,1:T(8,128)(2,1)S(1)} %slice.269), channel_id=1, source_target_pairs={{4,0},{8,4},{12,8},{5,1},{9,5},{13,9},{6,2},{10,6},{14,10},{7,3},{... | collective-permute-start | bytes 196616 | tf_op jit(solution)/shard_map/ppermute | solution.py:17
  15.3 143.3 %collective-permute-start = (bf16[128,4,64]{0,2,1:T(8,128)(2,1)S(1)}, bf16[128,4,64]{0,2,1:T(8,128)(2,1)S(1)}, u32[]{:S(2)}, u32[]{:S(2)}) collective-permute-start(bf16[128,4,64]{0,2,1:T(8,128)(2,1)S(1)} %slice.268), channel_id=1, source_target_pairs={{0,4},{4,8},{8,12},{1,5},{5,9},{9,13},{2,6},{6,10},{10,14},{3,7},{... | collective-permute-start | bytes 196616 | tf_op jit(solution)/shard_map/ppermute | solution.py:17
  25.6 7.2 copy-start
  195.2 7.9 %copy-start.1 = (bf16[4,64,512]{2,1,0:T(8,128)(2,1)S(1)}, bf16[4,64,512]{2,1,0:T(8,128)(2,1)}, u32[]{:S(2)}) copy-start(bf16[4,64,512]{2,1,0:T(8,128)(2,1)} %reshape.107) | copy-start | bytes 786436 | tf_op jit(solution)/shard_map/while
  252.6 7.9 %copy-start.1 = (bf16[4,64,512]{2,1,0:T(8,128)(2,1)S(1)}, bf16[4,64,512]{2,1,0:T(8,128)(2,1)}, u32[]{:S(2)}) copy-start(bf16[4,64,512]{2,1,0:T(8,128)(2,1)} %reshape.107) | copy-start | bytes 786436 | tf_op jit(solution)/shard_map/while
  323.4 7.9 %copy-start.1 = (bf16[4,64,512]{2,1,0:T(8,128)(2,1)S(1)}, bf16[4,64,512]{2,1,0:T(8,128)(2,1)}, u32[]{:S(2)}) copy-start(bf16[4,64,512]{2,1,0:T(8,128)(2,1)} %reshape.107) | copy-start | bytes 786436 | tf_op jit(solution)/shard_map/while
  394.2 7.9 %copy-start.1 = (bf16[4,64,512]{2,1,0:T(8,128)(2,1)S(1)}, bf16[4,64,512]{2,1,0:T(8,128)(2,1)}, u32[]{:S(2)}) copy-start(bf16[4,64,512]{2,1,0:T(8,128)(2,1)} %reshape.107) | copy-start | bytes 786436 | tf_op jit(solution)/shard_map/while
  435.5 268.7 %all-reduce.3.cloned.1.call-start = ((), (), s32[]{:S(2)}) async-start(), calls=%async_computation.2 | async-start | bytes 8388608 | tf_op jit(solution)/shard_map/psum | solution.py:114
Sparse Core Ops, SparseCore 0:
  435.7 10.2 reduce-scatter.1
Sparse Core Ops, SparseCore 1:
  548.6 155.6 all-reduce.2
where the time goes:
time: 755 us; the launch traced here: 750 us
  local copies, waits for them, and re-layouts  365 us (48%)
  waiting for transfers between devices  154 us (20%)
  matrix products  131 us (17%)
  other arithmetic  40.7 us (5%)
  blocking collectives  31.9 us (4%)
  between operations  17 us (2%)
    psum x1, waiting for transfers between devices, local(): grad_sum = lax.psum(grad_flat, 'tm')  154 us
    dot_general x4, matrix products, advance(): jnp.einsum('bkx,bky->bxy', row_block, earlier, preferred_element_type=jnp...  96.3 us
    while x72, local copies, waits for them, and re-layouts  56.9 us
    reshape x1, local copies, waits for them, and re-layouts, local(): grad_total.reshape(local_bundles, tile_rows, bundle_width, lag_count + ti...  54.3 us
    another operation x2, local copies, waits for them, and re-layouts, local(): jnp.stack([kernel_pad[:, tile_rows - shift_row:tile_rows - shift_row + la...  50.8 us
    reshape x8, local copies, waits for them, and re-layouts, tiles_of(): return wide.reshape(bundles, tile_count, (lag_count + tile_rows) * width)  49.2 us
    reshape x1, local copies, waits for them, and re-layouts, local(): toeplitz.reshape(local_bundles, (lag_count + tile_rows) * bundle_width, t...  49.1 us
    unnamed x16, local copies, waits for them, and re-layouts  35.8 us
  transfers between devices with their start and end apart: 4, of which 1 were waited for; matrix products, arithmetic and copies ran while one was open for 34% of the time, Pallas kernels for 0%

commit v1 on v0

--- a/solution.py
+++ b/solution.py
@@ -111,7 +111,7 @@
         jnp.bfloat16
     )
     grad_flat = grad_blocks.reshape(local_bundles, lag_count, bundle_width * bundle_width)
-    grad_sum = lax.psum(grad_flat, "tm")
+    grad_sum = jnp.sum(lax.all_gather(grad_flat, "tm"), axis=0)
     share_cols = grad_flat.shape[2] // lax.axis_size("tm")
     own_grad = lax.dynamic_slice_in_dim(grad_sum, lax.axis_index("tm") * share_cols, share_cols, 2)
     own_squares = jnp.sum(own_grad * own_grad)

time: 755 us -> 896 us (1.19)
  waiting for transfers between devices: 154 us -> 286 us
  other arithmetic: 40.7 us -> 50.5 us
    all_gather x0 -> x1, waiting for transfers between devices: none -> 286 us  [local(): grad_sum = jnp.sum(lax.all_gather(grad_flat, 'tm'), axis=0)]
    psum x1 -> x0, waiting for transfers between devices: 154 us -> none  [local(): grad_sum = lax.psum(grad_flat, 'tm')]
    reduce_sum x0 -> x1, other arithmetic: none -> 9.83 us  [local(): grad_sum = jnp.sum(lax.all_gather(grad_flat, 'tm'), axis=0)]
  transfers between devices with their start and end apart: 4 -> 4, of which waited for: 1 -> 1; matrix products, arithmetic and copies ran while one was open for 34% -> 28% of each run, Pallas kernels for 0% -> 0%
where the time goes in v1:
time: 896 us; the launch traced here: 890 us
  local copies, waits for them, and re-layouts  365 us (41%)
  waiting for transfers between devices  286 us (32%)
  matrix products  131 us (15%)
  other arithmetic  50.5 us (6%)
  blocking collectives  31.1 us (3%)
  between operations  17 us (2%)
    all_gather x1, waiting for transfers between devices, local(): grad_sum = jnp.sum(lax.all_gather(grad_flat, 'tm'), axis=0)  286 us
    dot_general x4, matrix products, advance(): jnp.einsum('bkx,bky->bxy', row_block, earlier, preferred_element_type=jnp...  96.3 us
    while x72, local copies, waits for them, and re-layouts  56.9 us
    reshape x1, local copies, waits for them, and re-layouts, local(): grad_total.reshape(local_bundles, tile_rows, bundle_width, lag_count + ti...  54.3 us
    another operation x2, local copies, waits for them, and re-layouts, local(): jnp.stack([kernel_pad[:, tile_rows - shift_row:tile_rows - shift_row + la...  50.8 us
    reshape x8, local copies, waits for them, and re-layouts, tiles_of(): return wide.reshape(bundles, tile_count, (lag_count + tile_rows) * width)  49.2 us
    reshape x1, local copies, waits for them, and re-layouts, local(): toeplitz.reshape(local_bundles, (lag_count + tile_rows) * bundle_width, t...  49.1 us
    unnamed x16, local copies, waits for them, and re-layouts  35.8 us
  transfers between devices with their start and end apart: 4, of which 1 were waited for; matrix products, arithmetic and copies ran while one was open for 28% of the time, Pallas kernels for 0%

profile of v1, /device:TPU:0, one launch (start us, length us, event | category | flops | bytes accessed | tf_op | source)
XLA Modules:
  0.0 890.5 jit_solution(18398430776943319287)
XLA Ops:
  59.8 47.4 %copy.43 = bf16[4,72,64,8,64]{4,3,2,1,0:T(8,128)(2,1)} copy(bf16[4,72,64,8,64]{1,4,3,2,0:T(8,128)(2,1)} %fusion.1) | data formatting | bytes 37748736 | tf_op jit(solution)/shard_map/stack | solution.py:59
  107.2 49.1 %reshape.89 = bf16[4,4608,512]{2,1,0:T(8,128)(2,1)} reshape(bf16[4,72,64,8,64]{4,3,2,1,0:T(8,128)(2,1)} %copy.43) | data formatting | bytes 37748736 | tf_op jit(solution)/shard_map/reshape | solution.py:66
  159.7 269.9 %while.17 = (s32[]{:T(128)}, f32[4,512,4608]{2,1,0:T(8,128)}, f32[4,4,512,64]{3,2,1,0:T(8,128)}, s32[4]{0:T(128)S(1)}, bf16[4,2048,64]{1,2,0:T(8,128)(2,1)}, /*i...) while((s32[]{:T(128)}, f32[4,512,4608]{2,1,0:T(8,128)}, ...), condition=%wide.region_1.2_spmd.clone, body=%wide.region_0.1_spmd.clone.sunk | while | flops 2434793472 | bytes 131072384 | solution.py:92
  173.4 6.1 reshape.105
  179.5 8.1 fusion.24
  196.9 6.1 reshape.104
  203.1 14.0 %select_add_fusion.2 = f32[4,512,4608]{2,1,0:T(8,128)} fusion(f32[4,512,4608]{2,1,0:T(8,128)} %get-tuple-element.342, pred[]{:T(512)S(6)} %compare.4, bf16[4,64,512]{2,1,0:T(8,128)(2,1)S(1)} %copy-done.1, bf16[4,64,4608]{2,1,0:T(8,128)(2,1)S(1)} %reshape.104), kind=kOutput, calls=%fused_computation.clone.1 | convolution fusion | flops 1226833920 | bytes 78118912 | tf_op jit(solution)/shard_map/while/body/eval_jaxpr/bkx,bky->bxy/dot_general | solution.py:86
  230.8 6.1 reshape.105
  236.9 8.1 fusion.24
  254.4 6.1 reshape.104
  260.5 27.4 %select_add_fusion.2 = f32[4,512,4608]{2,1,0:T(8,128)} fusion(f32[4,512,4608]{2,1,0:T(8,128)} %get-tuple-element.342, pred[]{:T(512)S(6)} %compare.4, bf16[4,64,512]{2,1,0:T(8,128)(2,1)S(1)} %copy-done.1, bf16[4,64,4608]{2,1,0:T(8,128)(2,1)S(1)} %reshape.104), kind=kOutput, calls=%fused_computation.clone.1 | convolution fusion | flops 1226833920 | bytes 78118912 | tf_op jit(solution)/shard_map/while/body/eval_jaxpr/bkx,bky->bxy/dot_general | solution.py:86
  307.8 8.1 fusion.24
  331.4 27.4 %select_add_fusion.2 = f32[4,512,4608]{2,1,0:T(8,128)} fusion(f32[4,512,4608]{2,1,0:T(8,128)} %get-tuple-element.342, pred[]{:T(512)S(6)} %compare.4, bf16[4,64,512]{2,1,0:T(8,128)(2,1)S(1)} %copy-done.1, bf16[4,64,4608]{2,1,0:T(8,128)(2,1)S(1)} %reshape.104), kind=kOutput, calls=%fused_computation.clone.1 | convolution fusion | flops 1226833920 | bytes 78118912 | tf_op jit(solution)/shard_map/while/body/eval_jaxpr/bkx,bky->bxy/dot_general | solution.py:86
  378.6 8.1 fusion.24
  396.0 6.1 reshape.104
  402.2 27.4 %select_add_fusion.2 = f32[4,512,4608]{2,1,0:T(8,128)} fusion(f32[4,512,4608]{2,1,0:T(8,128)} %get-tuple-element.342, pred[]{:T(512)S(6)} %compare.4, bf16[4,64,512]{2,1,0:T(8,128)(2,1)S(1)} %copy-done.1, bf16[4,64,4608]{2,1,0:T(8,128)(2,1)S(1)} %reshape.104), kind=kOutput, calls=%fused_computation.clone.1 | convolution fusion | flops 1226833920 | bytes 78118912 | tf_op jit(solution)/shard_map/while/body/eval_jaxpr/bkx,bky->bxy/dot_general | solution.py:86
  435.6 54.3 %reshape.91 = f32[4,8,64,72,64]{4,3,2,1,0:T(8,128)} reshape(f32[4,512,4608]{2,1,0:T(8,128)} %get-tuple-element.183) | data formatting | bytes 75497472 | tf_op jit(solution)/shard_map/reshape | solution.py:98
  489.9 27.4 %fusion = f32[4,64,64,64]{3,2,1,0:T(8,128)} fusion(f32[4,8,64,72,64]{4,3,2,1,0:T(8,128)} %reshape.91), kind=kLoop, calls=%fused_computation.24 | loop fusion | flops 7340032 | bytes 37748736 | tf_op jit(solution)/shard_map/add | solution.py:103
  517.3 11.9 %rev.4 = f32[4,64,64,64]{3,2,1,0:T(8,128)} reverse(f32[4,64,64,64]{3,2,1,0:T(8,128)} %fusion), dimensions={2} | reverse | bytes 8388608 | tf_op jit(solution)/shard_map/jit(_flip)/rev | solution.py:104
  529.1 11.5 %copy.48 = f32[4,64,64,64]{3,2,1,0:T(8,128)} copy(f32[4,64,64,64]{3,1,2,0:T(8,128)} %bitcast.113) | data formatting | bytes 8388608 | tf_op jit(solution)/shard_map/transpose | solution.py:104
  540.6 7.9 all_gather_reshape.3
  549.9 286.1 %all-gather.2.cloned.1.call-done = f32[4,4,64,4096]{3,2,1,0:T(8,128)} async-done(((f32[1,4,64,4096]{3,2,1,0:T(8,128)}), f32[4,4,64,4096]{3,2,1,0:T(8,128)}) %all-gather.2.cloned.1.call-update) | async-done | bytes 16777232 | tf_op jit(solution)/shard_map/all_gather | solution.py:114
  836.0 9.8 %reduce_sum.18 = f32[4,64,4096]{2,1,0:T(8,128)} reduce(f32[4,4,64,4096]{3,2,1,0:T(8,128)} %all-gather.2.cloned.1.call-done, f32[]{:T(128)} %constant.91.clone.1), dimensions={0}, to_apply=%region_3.4 | reduce | flops 3145728 | bytes 20971524 | tf_op jit(solution)/shard_map/reduce_sum | solution.py:114
  848.9 31.1 %psum.7 = f32[]{:T(128)} all-reduce(f32[]{:T(128)} %multiply_reduce_fusion), channel_id=1, replica_groups=mesh['case'=2,'tm'=4,'bundle'=2,'sub'=2] {'tm','bundle','sub'}, use_global_device_ids=true, to_apply=%region_5.6 | all-reduce | flops 1 | bytes 8 | tf_op jit(solution)/shard_map/psum | solution.py:118
  (162 shorter events, 174.6 us)
Async XLA Ops:
  8.0 6.5 copy-start.2
  8.0 540.5 %reduce-scatter.2.cloned.1.call-start = ((), (), s32[]{:S(2)}) async-start(), calls=%async_computation.1 | async-start | bytes 3145728 | tf_op jit(solution)/shard_map/reduce_scatter | solution.py:105
  12.5 143.7 %collective-permute-start.1 = (bf16[128,4,64]{0,2,1:T(8,128)(2,1)S(1)}, bf16[128,4,64]{0,2,1:T(8,128)(2,1)S(1)}, u32[]{:S(2)}, u32[]{:S(2)}) collective-permute-start(bf16[128,4,64]{0,2,1:T(8,128)(2,1)S(1)} %slice.269), channel_id=1, source_target_pairs={{4,0},{8,4},{12,8},{5,1},{9,5},{13,9},{6,2},{10,6},{14,10},{7,3},{... | collective-permute-start | bytes 196616 | tf_op jit(solution)/shard_map/ppermute | solution.py:17
  15.3 143.3 %collective-permute-start = (bf16[128,4,64]{0,2,1:T(8,128)(2,1)S(1)}, bf16[128,4,64]{0,2,1:T(8,128)(2,1)S(1)}, u32[]{:S(2)}, u32[]{:S(2)}) collective-permute-start(bf16[128,4,64]{0,2,1:T(8,128)(2,1)S(1)} %slice.268), channel_id=1, source_target_pairs={{0,4},{4,8},{8,12},{1,5},{5,9},{9,13},{2,6},{6,10},{10,14},{3,7},{... | collective-permute-start | bytes 196616 | tf_op jit(solution)/shard_map/ppermute | solution.py:17
  25.6 7.2 copy-start
  195.2 7.9 copy-start.1
  252.6 7.9 copy-start.1
  323.4 7.9 copy-start.1
  394.2 7.9 copy-start.1
  435.5 400.5 %all-gather.2.cloned.1.call-start = ((), (), s32[]{:S(2)}) async-start(), calls=%async_computation.2 | async-start | bytes 20971520 | tf_op jit(solution)/shard_map/all_gather | solution.py:114
Sparse Core Ops, SparseCore 0:
  435.7 10.2 reduce-scatter.1
Sparse Core Ops, SparseCore 1:
  548.6 287.4 all-gather.1
